TPU v7x, 512 devices: a whole 4x4x16 slice. The times are simulated.
512 devices in a mesh: req: 128 (over y, z, core), tp: 4 (over x).
Axes of the slice: x: 4, y: 4, z: 16, core: 2. Of those that a mesh axis runs over, the one named last changes fastest.
Arguments:
- tokens: bfloat16 [131072, 3584], P('req', 'tp'), may hold values from -6 to 6
- key_value_weight: bfloat16 [3584, 1024], P('tp'), may hold values from -0.09375 to 0.09375
- adapter_down_maps: bfloat16 [128, 16, 3584], P('req', None, 'tp'), may hold values from -0.09375 to 0.09375
- adapter_up_maps: bfloat16 [128, 16, 1024], P('req', None, 'tp'), may hold values from -1.5 to 1.5
- block_adapter_ids: int32 [1024], P('req'), may hold values from 0 to 127, never falling along the last dimension, each value on 1 to 32 neighbouring positions
- block_live_rows: int32 [1024], P('req'), may hold values from 32 to 128
- adapter_storage_slot: int32 [128], replicated, may hold values from 0 to 127, each once
Outputs:
- keys_values: bfloat16 [131072, 1024], P('req', 'tp')
Inputs may be any that keep to these rules, and one draw needn't show every extreme that they name: `block_adapter_ids`: block ids never fall from one block to the next, every adapter id names at least one block, and one adapter names 32 blocks. `adapter_storage_slot`: each storage slot belongs to exactly one adapter.
All inputs are finite; a program needn't handle non-finite values.
Results may differ from a plain program's by a relative error of at most 0.003.
Values may be sent and summed in bfloat16 or wider, within the bound.
No kernel may reach another device: no remote copies, remote signals or barrier semaphores. Data moves between devices by JAX's collectives and lax.ppermute only.
A program may use at most 64 MiB of HBM per device.

v0:
```python
import numpy as np
import jax
import jax.numpy as jnp
from jax import lax
from jax.experimental.layout import Layout, with_layout_constraint
from jax.sharding import Mesh
from jax.sharding import PartitionSpec as P

adapter_scale = 0.5
ROWS = ("y", "z", "c")


def pick_entries(table, wanted, own_row, own_column, per_row, per_column):
    row_of = wanted // per_row
    inside = wanted % per_row
    entries = table[(own_column - inside % per_column) % per_column, inside // per_column]
    keep = (row_of == own_row)[:, None, None]
    return jnp.where(keep, entries, jnp.zeros_like(entries))


def shards(
    tokens,
    key_value_weight,
    adapter_down_maps,
    adapter_up_maps,
    block_adapter_ids,
    block_live_rows,
    adapter_storage_slot,
):
    rows_dev, width_dev = tokens.shape
    blocks_dev = block_adapter_ids.shape[0]
    block_rows = rows_dev // blocks_dev
    rank = adapter_down_maps.shape[1]
    local_columns = adapter_up_maps.shape[2]
    tp_size = key_value_weight.shape[1] // local_columns
    y_size = lax.axis_size("y")
    per_column = lax.axis_size("c")
    per_row = lax.axis_size("z") * per_column
    slot_ids = adapter_storage_slot[block_adapter_ids]
    my_row = lax.axis_index("y")
    base_partial = jnp.dot(tokens, key_value_weight, preferred_element_type=jnp.float32)
    outgoing = base_partial.reshape(rows_dev, tp_size, local_columns).transpose(1, 0, 2)
    incoming = lax.all_to_all(outgoing, "tp", 0, 0, tiled=False)
    both_maps = jnp.concatenate([adapter_down_maps, adapter_up_maps], axis=2)
    both_maps, outgoing = lax.optimization_barrier((both_maps, outgoing))
    column = lax.all_gather(both_maps, "z", axis=0, tiled=True)
    c_size = lax.axis_size("c")
    row_table = jnp.stack(
        [column]
        + [
            lax.ppermute(column, "c", [(i, (i + shift) % c_size) for i in range(c_size)])
            for shift in range(1, c_size)
        ]
    )
    row_ids = lax.all_to_all(
        jnp.broadcast_to(slot_ids[None], (y_size, blocks_dev)), "y", 0, 0, tiled=False
    )
    row_table, incoming = lax.optimization_barrier((row_table, incoming))
    base_result = with_layout_constraint(jnp.sum(incoming, axis=0), Layout((0, 1)))
    sent = pick_entries(
        row_table, row_ids.reshape(-1), my_row, lax.axis_index("c"), per_row, per_column
    )
    received = lax.all_to_all(
        sent.reshape((y_size, blocks_dev) + sent.shape[1:]), "y", 0, 0, tiled=False
    )
    received, base_result = lax.optimization_barrier((received, base_result))
    chosen_maps = jnp.sum(received, axis=0, dtype=received.dtype)
    chosen_down_maps = chosen_maps[:, :, :width_dev]
    chosen_up_maps = chosen_maps[:, :, width_dev:]
    blocked_input = tokens.reshape(blocks_dev, block_rows, width_dev)
    shrunk_partial = jnp.einsum(
        "qzo,qjo->qzj", blocked_input, chosen_down_maps, preferred_element_type=jnp.float32
    ).reshape(rows_dev, rank)
    shrunk = jnp.sum(
        lax.all_to_all(
            jnp.broadcast_to(shrunk_partial[None], (tp_size,) + shrunk_partial.shape),
            "tp",
            0,
            0,
            tiled=False,
        ),
        axis=0,
    )
    low_values = shrunk.astype(jnp.bfloat16)
    adapter_result = jnp.einsum(
        "bkr,brc->bkc",
        low_values.reshape(blocks_dev, block_rows, rank),
        chosen_up_maps,
        preferred_element_type=jnp.float32,
    ).reshape(rows_dev, local_columns)
    live_rows = (
        jnp.arange(block_rows, dtype=jnp.int32)[None, :] < block_live_rows[:, None]
    ).reshape(rows_dev, 1)
    adapted_output = base_result + adapter_scale * adapter_result
    return jnp.where(live_rows, adapted_output, jnp.zeros_like(adapted_output)).astype(jnp.bfloat16)


def split_mesh(mesh):
    devices = np.asarray(mesh.devices)
    first = devices[:, 0]
    y_size = len({d.coords[1] for d in first})
    z_size = len({d.coords[2] for d in first})
    c_size = len({d.core_on_chip for d in first})
    split = devices.reshape(y_size, z_size, c_size, devices.shape[1])
    for (yi, zi, ci), d in np.ndenumerate(split[:, :, :, 0]):
        assert (d.coords[1], d.coords[2], d.core_on_chip) == (
            sorted({e.coords[1] for e in first})[yi],
            sorted({e.coords[2] for e in first})[zi],
            sorted({e.core_on_chip for e in first})[ci],
        )
    return Mesh(split, ROWS + ("tp",))


def solution(mesh):
    in_specs = (
        P(ROWS, "tp"),
        P("tp", None),
        P(ROWS, None, "tp"),
        P(ROWS, None, "tp"),
        P(ROWS),
        P(ROWS),
        P(),
    )
    out_specs = P(ROWS, "tp")
    return jax.shard_map(
        shards, mesh=split_mesh(mesh), in_specs=in_specs, out_specs=out_specs, check_vma=False
    )
```

profile of v0, /device:TPU:416, one launch (start us, length us, event | category | flops | bytes accessed | tf_op | source)
XLA Modules:
  0.0 102.7 jit_solution(1394720287949011068)
XLA Ops:
  0.0 0.0 copy-start
  0.0 0.8 compare_select_fusion.2
  0.8 1.3 %gather_fusion = s32[8]{0:T(128)S(1)} fusion(s32[128]{0:T(128)} %param.13, s32[1024]{0:T(1024)S(1)} %pad_clamp_fusion), kind=kCustom, calls=%fused_computation | custom fusion | bytes 96 | tf_op jit(solution)/shard_map/gather | solution.py:39
  2.1 0.6 broadcast_in_dim.45
  2.7 4.5 %all-to-all-start = ((s32[4,1,8]{2,1,0:T(1,128)}), s32[4,1,8]{2,1,0:T(1,128)S(1)}, u32[]{:S(2)}, u32[]{:S(2)}) async-start(s32[4,1,8]{2,1,0:T(1,128)} %broadcast_in_dim.45), calls=%async_computation | async-start | bytes 4096 | tf_op jit(solution)/shard_map/all_to_all | solution.py:55
  7.2 0.0 copy-done
  7.2 5.9 %fusion.19 = f32[1024,1024]{0,1:T(8,128)} fusion(bf16[1024,896]{1,0:T(8,128)(2,1)S(1)} %copy-done, bf16[896,1024]{1,0:T(8,128)(2,1)} %param.8), kind=kOutput, calls=%fused_computation.50 | convolution fusion | flops 1879048192 | bytes 7864320 | tf_op jit(solution)/shard_map/dot_general | solution.py:41
  13.0 0.0 all-to-all-done
  13.0 5.0 %all-to-all-start.1 = ((f32[4,1024,256]{1,2,0:T(8,128)}), f32[4,1024,256]{1,2,0:T(8,128)}, u32[]{:S(2)}, u32[]{:S(2)}) async-start(f32[4,1024,256]{1,2,0:T(8,128)} %bitcast.38), calls=%async_computation.1 | async-start | bytes 8388608 | tf_op jit(solution)/shard_map/all_to_all | solution.py:43
  18.0 30.4 %all_gather.3 = bf16[16,16,1152]{2,1,0:T(8,128)(2,1)S(1)} all-gather(bf16[1,16,1152]{2,1,0:T(8,128)(2,1)S(1)} %pad_maximum_fusion.1), channel_id=1, replica_groups=mesh['y'=4,'z'=16,'c'=2,'tp'=4] {'z'}, dimensions={0}, use_global_device_ids=true | all-gather | bytes 626688 | tf_op jit(solution)/shard_map/all_gather | solution.py:46
  48.5 1.9 %collective-permute-start = (bf16[16,16,1152]{2,1,0:T(8,128)(2,1)S(1)}, bf16[16,16,1152]{2,1,0:T(8,128)(2,1)S(1)}, u32[]{:S(2)}, u32[]{:S(2)}) collective-permute-start(bf16[16,16,1152]{2,1,0:T(8,128)(2,1)S(1)} %all_gather.3), channel_id=1, source_target_pairs={{0,4},{4,0},{1,5},{5,1},{2,6},{6,2},{3,7},{7,3},{8,12},{12,8},{9,1... | collective-permute-start | bytes 1769480 | tf_op jit(solution)/shard_map/ppermute | solution.py:51
  50.4 0.5 broadcast.294
  50.9 0.7 reduce.3
  51.6 0.1 reshape.258
  51.7 0.6 collective-permute-done
  52.4 1.2 %pad_maximum_fusion = bf16[2,16,16,1152]{3,2,1,0:T(8,128)(2,1)} fusion(bf16[1,16,16,1152]{3,2,1,0:T(8,128)(2,1)S(1)} %bitcast.40, bf16[1,16,16,1152]{3,2,1,0:T(8,128)(2,1)S(1)} %bitcast.39), kind=kLoop, calls=%fused_computation.3 | loop fusion | flops 589824 | bytes 2359296 | tf_op jit(solution)/shard_map/stack | solution.py:48
  53.6 13.3 %all-to-all-done.1 = f32[4,1024,256]{1,2,0:T(8,128)} async-done(((f32[4,1024,256]{1,2,0:T(8,128)}), f32[4,1024,256]{1,2,0:T(8,128)}, u32[]{:S(2)}, u32[]{:S(2)}) %all-to-all-start.1) | async-done | bytes 4194336 | tf_op jit(solution)/shard_map/all_to_all | solution.py:43
  66.9 2.0 %gather_fusion.1 = bf16[32,16,1152]{2,1,0:T(8,128)(2,1)S(1)} fusion(bf16[2,16,16,1152]{3,2,1,0:T(8,128)(2,1)} %pad_maximum_fusion, s32[32]{0:T(128)S(1)} %fusion.18), kind=kCustom, calls=%fused_computation.1 | custom fusion | bytes 2359552 | tf_op jit(solution)/shard_map/gather | solution.py:16
  68.9 1.2 %broadcast_select_fusion = bf16[4,8,16,1152]{3,2,1,0:T(8,128)(2,1)} fusion(bf16[4,8,16,1152]{3,2,1,0:T(8,128)(2,1)S(1)} %bitcast.37, pred[4,8]{1,0:T(4,128)(4,1)S(1)} %fusion.8), kind=kLoop, calls=%fused_computation.4 | loop fusion | flops 589824 | bytes 2359328 | tf_op jit(solution)/shard_map/jit(_where)/select_n | solution.py:18
  70.1 4.5 %all-to-all-start.2 = ((bf16[4,8,16,1152]{3,2,1,0:T(8,128)(2,1)}), bf16[4,8,16,1152]{3,2,1,0:T(8,128)(2,1)S(1)}, u32[]{:S(2)}, u32[]{:S(2)}) async-start(bf16[4,8,16,1152]{3,2,1,0:T(8,128)(2,1)} %broadcast_select_fusion), calls=%async_computation.2 | async-start | bytes 2359296 | tf_op jit(solution)/shard_map/all_to_all | solution.py:63
  74.6 3.7 %reduce_sum.27 = f32[1024,256]{0,1:T(8,128)} reduce(f32[4,1024,256]{1,2,0:T(8,128)} %all-to-all-done.1, f32[]{:T(128)} %constant.75.clone.1), dimensions={0}, to_apply=%region_0.0 | reduce | flops 786432 | bytes 5242884 | tf_op jit(solution)/shard_map/reduce_sum | solution.py:59
  78.3 2.5 %copy.11 = f32[1024,256]{1,0:T(8,128)} copy(f32[1024,256]{0,1:T(8,128)} %reduce_sum.27) | data formatting | bytes 2097152 | tf_op jit(solution)/shard_map/reduce_sum | solution.py:59
  80.8 8.8 %all-to-all-done.2 = bf16[4,8,16,1152]{3,2,1,0:T(8,128)(2,1)S(1)} async-done(((bf16[4,8,16,1152]{3,2,1,0:T(8,128)(2,1)}), bf16[4,8,16,1152]{3,2,1,0:T(8,128)(2,1)S(1)}, u32[]{:S(2)}, u32[]{:S(2)}) %all-to-all-start.2) | async-done | bytes 1179680 | tf_op jit(solution)/shard_map/all_to_all | solution.py:63
  89.7 0.2 reduce_sum.28
  89.9 0.0 copy-start.4
  89.9 0.6 convolution_bitcast_fusion
  90.5 0.7 broadcast_in_dim.49
  91.3 3.4 %all-to-all-start.3 = ((f32[4,1024,16]{1,2,0:T(8,128)}), f32[4,1024,16]{1,2,0:T(8,128)S(1)}, u32[]{:S(2)}, u32[]{:S(2)}) async-start(f32[4,1024,16]{1,2,0:T(8,128)} %broadcast_in_dim.49), calls=%async_computation.3 | async-start | bytes 524288 | tf_op jit(solution)/shard_map/all_to_all | solution.py:75
  94.7 0.1 fusion.6
  94.8 6.6 %all-to-all-done.3 = f32[4,1024,16]{1,2,0:T(8,128)S(1)} async-done(((f32[4,1024,16]{1,2,0:T(8,128)}), f32[4,1024,16]{1,2,0:T(8,128)S(1)}, u32[]{:S(2)}, u32[]{:S(2)}) %all-to-all-start.3) | async-done | bytes 262176 | tf_op jit(solution)/shard_map/all_to_all | solution.py:75
  101.3 0.3 convolution_multiply_fusion
  101.7 1.0 %fusion.1 = bf16[1024,256]{1,0:T(8,128)(2,1)} fusion(f32[1024,256]{1,0:T(8,128)S(1)} %copy-done.1, f32[8,128,256]{2,1,0:T(8,128)S(1)} %convolution_multiply_fusion, pred[1024]{0:T(1024)(128)(4,1)S(1)} %fusion.6), kind=kLoop, calls=%fused_computation.8 | loop fusion | flops 786432 | bytes 2622464 | tf_op jit(solution)/shard_map/convert_element_type | solution.py:95
  (13 shorter events, 0.1 us)
Async XLA Ops:
  0.0 7.2 %copy-start = (bf16[1024,896]{1,0:T(8,128)(2,1)S(1)}, bf16[1024,896]{1,0:T(8,128)(2,1)}, u32[]{:S(2)}) copy-start(bf16[1024,896]{1,0:T(8,128)(2,1)} %param.7) | copy-start | bytes 5505028
  2.7 10.3 %all-to-all-start = ((s32[4,1,8]{2,1,0:T(1,128)}), s32[4,1,8]{2,1,0:T(1,128)S(1)}, u32[]{:S(2)}, u32[]{:S(2)}) async-start(s32[4,1,8]{2,1,0:T(1,128)} %broadcast_in_dim.45), calls=%async_computation | async-start | bytes 4096 | tf_op jit(solution)/shard_map/all_to_all | solution.py:55
  13.0 5.0 %copy-start.2 = (bf16[1,16,896]{2,1,0:T(8,128)(2,1)S(1)}, bf16[1,16,896]{2,1,0:T(8,128)(2,1)}, u32[]{:S(2)}) copy-start(bf16[1,16,896]{2,1,0:T(8,128)(2,1)} %param.9) | copy-start | bytes 86020
  13.0 5.0 %copy-start.3 = (bf16[1,16,256]{2,1,0:T(8,128)(2,1)S(1)}, bf16[1,16,256]{2,1,0:T(8,128)(2,1)}, u32[]{:S(2)}) copy-start(bf16[1,16,256]{2,1,0:T(8,128)(2,1)} %param.10) | copy-start | bytes 24580
  13.0 53.8 %all-to-all-start.1 = ((f32[4,1024,256]{1,2,0:T(8,128)}), f32[4,1024,256]{1,2,0:T(8,128)}, u32[]{:S(2)}, u32[]{:S(2)}) async-start(f32[4,1024,256]{1,2,0:T(8,128)} %bitcast.38), calls=%async_computation.1 | async-start | bytes 8388608 | tf_op jit(solution)/shard_map/all_to_all | solution.py:43
  48.5 3.9 %collective-permute-start = (bf16[16,16,1152]{2,1,0:T(8,128)(2,1)S(1)}, bf16[16,16,1152]{2,1,0:T(8,128)(2,1)S(1)}, u32[]{:S(2)}, u32[]{:S(2)}) collective-permute-start(bf16[16,16,1152]{2,1,0:T(8,128)(2,1)S(1)} %all_gather.3), channel_id=1, source_target_pairs={{0,4},{4,0},{1,5},{5,1},{2,6},{6,2},{3,7},{7,3},{8,12},{12,8},{9,1... | collective-permute-start | bytes 1769480 | tf_op jit(solution)/shard_map/ppermute | solution.py:51
  70.1 19.6 %all-to-all-start.2 = ((bf16[4,8,16,1152]{3,2,1,0:T(8,128)(2,1)}), bf16[4,8,16,1152]{3,2,1,0:T(8,128)(2,1)S(1)}, u32[]{:S(2)}, u32[]{:S(2)}) async-start(bf16[4,8,16,1152]{3,2,1,0:T(8,128)(2,1)} %broadcast_select_fusion), calls=%async_computation.2 | async-start | bytes 2359296 | tf_op jit(solution)/shard_map/all_to_all | solution.py:63
  89.9 4.8 %copy-start.4 = (s32[8]{0:T(128)S(1)}, s32[8]{0:T(128)}, u32[]{:S(2)}) copy-start(s32[8]{0:T(128)} %param.12) | copy-start | bytes 100
  89.9 11.8 %copy-start.1 = (f32[1024,256]{1,0:T(8,128)S(1)}, f32[1024,256]{1,0:T(8,128)}, u32[]{:S(2)}) copy-start(f32[1024,256]{1,0:T(8,128)} %copy.11) | copy-start | bytes 3145732
  91.3 10.1 %all-to-all-start.3 = ((f32[4,1024,16]{1,2,0:T(8,128)}), f32[4,1024,16]{1,2,0:T(8,128)S(1)}, u32[]{:S(2)}, u32[]{:S(2)}) async-start(f32[4,1024,16]{1,2,0:T(8,128)} %broadcast_in_dim.49), calls=%async_computation.3 | async-start | bytes 524288 | tf_op jit(solution)/shard_map/all_to_all | solution.py:75
where the time goes:
time: 103 us
  blocking collectives  30.4 us (30%)
  waiting for transfers between devices  29.3 us (28%)
  starting transfers between devices  19.3 us (19%)
  other arithmetic  8.97 us (9%)
  local copies, waits for them, and re-layouts  7.78 us (8%)
  matrix products  6.85 us (7%)
    all_gather x1, blocking collectives, shards(): column = lax.all_gather(both_maps, 'z', axis=0, tiled=True)  30.4 us
    all_to_all x1, waiting for transfers between devices, shards(): incoming = lax.all_to_all(outgoing, 'tp', 0, 0, tiled=False)  13.3 us
    all_to_all x1, waiting for transfers between devices, shards(): lax.all_to_all(sent.reshape((y_size, blocks_dev) + sent.shape[1:]), 'y',...  8.83 us
    all_to_all x1, waiting for transfers between devices, shards(): lax.all_to_all(jnp.broadcast_to(shrunk_partial[None], (tp_size,) + shrunk...  6.56 us
    dot_general x1, matrix products, shards(): jnp.dot(tokens, key_value_weight, preferred_element_type=jnp.float32)  5.86 us
    all_to_all x1, starting transfers between devices, shards(): incoming = lax.all_to_all(outgoing, 'tp', 0, 0, tiled=False)  4.98 us
    all_to_all x1, starting transfers between devices, shards(): lax.all_to_all(sent.reshape((y_size, blocks_dev) + sent.shape[1:]), 'y',...  4.52 us
    all_to_all x1, starting transfers between devices, shards(): lax.all_to_all(jnp.broadcast_to(slot_ids[None], (y_size, blocks_dev)), 'y...  4.46 us
  transfers between devices with their start and end apart: 5, of which 4 were waited for; matrix products, arithmetic and copies ran while one was open for 14% of the time, Pallas kernels for 0%

commit v1 on v0

--- a/solution.py
+++ b/solution.py
@@ -43,7 +43,9 @@
     incoming = lax.all_to_all(outgoing, "tp", 0, 0, tiled=False)
     both_maps = jnp.concatenate([adapter_down_maps, adapter_up_maps], axis=2)
     both_maps, outgoing = lax.optimization_barrier((both_maps, outgoing))
-    column = lax.all_gather(both_maps, "z", axis=0, tiled=True)
+    column = jnp.concatenate(
+        lax.all_to_all(jnp.stack([both_maps] * lax.axis_size("z")), "z", 0, 0), axis=0
+    )
     c_size = lax.axis_size("c")
     row_table = jnp.stack(
         [column]

time: 103 us -> 151 us (1.47)
  the two profiles are of different devices: /device:TPU:416 before, /device:TPU:32 now
where the time goes in v1:
time: 151 us; the launch traced here: 150 us
  waiting for transfers between devices  57.2 us (38%)
  blocking collectives  49.2 us (33%)
  starting transfers between devices  19.2 us (13%)
  other arithmetic  9.75 us (6%)
  local copies, waits for them, and re-layouts  7.84 us (5%)
  matrix products  6.84 us (5%)
    all_to_all x1, blocking collectives, shards(): lax.all_to_all(jnp.stack([both_maps] * lax.axis_size('z')), 'z', 0, 0)  49.2 us
    all_to_all x1, waiting for transfers between devices, shards(): incoming = lax.all_to_all(outgoing, 'tp', 0, 0, tiled=False)  42.3 us
    all_to_all x1, waiting for transfers between devices, shards(): lax.all_to_all(sent.reshape((y_size, blocks_dev) + sent.shape[1:]), 'y',...  7.71 us
    all_to_all x1, waiting for transfers between devices, shards(): lax.all_to_all(jnp.broadcast_to(shrunk_partial[None], (tp_size,) + shrunk...  6.56 us
    dot_general x1, matrix products, shards(): jnp.dot(tokens, key_value_weight, preferred_element_type=jnp.float32)  5.85 us
    all_to_all x1, starting transfers between devices, shards(): incoming = lax.all_to_all(outgoing, 'tp', 0, 0, tiled=False)  4.85 us
    all_to_all x1, starting transfers between devices, shards(): lax.all_to_all(sent.reshape((y_size, blocks_dev) + sent.shape[1:]), 'y',...  4.53 us
    all_to_all x1, starting transfers between devices, shards(): lax.all_to_all(jnp.broadcast_to(slot_ids[None], (y_size, blocks_dev)), 'y...  4.46 us
  transfers between devices with their start and end apart: 5, of which 4 were waited for; matrix products, arithmetic and copies ran while one was open for 10% of the time, Pallas kernels for 0%

profile of v1, /device:TPU:32, one launch (start us, length us, event | category | flops | bytes accessed | tf_op | source)
XLA Modules:
  0.0 150.1 jit_solution(6993332679952253321)
XLA Ops:
  0.0 0.8 compare_select_fusion.2
  0.8 1.3 gather_fusion
  2.1 0.6 broadcast_in_dim.45
  2.7 4.5 %all-to-all-start = ((s32[4,1,8]{2,1,0:T(1,128)}), s32[4,1,8]{2,1,0:T(1,128)S(1)}, u32[]{:S(2)}, u32[]{:S(2)}) async-start(s32[4,1,8]{2,1,0:T(1,128)} %broadcast_in_dim.45), calls=%async_computation | async-start | bytes 4096 | tf_op jit(solution)/shard_map/all_to_all | solution.py:57
  7.2 0.8 pad_maximum_fusion.1
  7.9 5.8 %fusion.19 = f32[1024,1024]{0,1:T(8,128)} fusion(bf16[1024,896]{1,0:T(8,128)(2,1)S(1)} %copy-done, bf16[896,1024]{1,0:T(8,128)(2,1)} %param.8), kind=kOutput, calls=%fused_computation.50 | convolution fusion | flops 1879048192 | bytes 7864320 | tf_op jit(solution)/shard_map/dot_general | solution.py:41
  13.8 0.0 all-to-all-done
  13.8 49.2 %all_to_all.26 = bf16[16,1,16,1152]{3,2,1,0:T(8,128)(2,1)S(1)} all-to-all(bf16[16,1,16,1152]{3,2,1,0:T(8,128)(2,1)S(1)} %stack.6), channel_id=1, replica_groups=mesh['y'=4,'z'=16,'c'=2,'tp'=4] {'z'}, dimensions={0} | all-to-all | bytes 1179648 | tf_op jit(solution)/shard_map/all_to_all | solution.py:47
  63.0 4.9 %all-to-all-start.2 = ((f32[4,1024,256]{1,2,0:T(8,128)}), f32[4,1024,256]{1,2,0:T(8,128)}, u32[]{:S(2)}, u32[]{:S(2)}) async-start(f32[4,1024,256]{1,2,0:T(8,128)} %bitcast.40), calls=%async_computation.2 | async-start | bytes 8388608 | tf_op jit(solution)/shard_map/all_to_all | solution.py:43
  67.9 1.9 %collective-permute-start = (bf16[16,16,1152]{2,1,0:T(8,128)(2,1)S(1)}, bf16[16,16,1152]{2,1,0:T(8,128)(2,1)S(1)}, u32[]{:S(2)}, u32[]{:S(2)}) collective-permute-start(bf16[16,16,1152]{2,1,0:T(8,128)(2,1)S(1)} %bitcast.41), channel_id=1, source_target_pairs={{0,4},{4,0},{1,5},{5,1},{2,6},{6,2},{3,7},{7,3},{8,12},{12,8},{9,1... | collective-permute-start | bytes 1769480 | tf_op jit(solution)/shard_map/ppermute | solution.py:53
  69.8 0.5 broadcast.297
  70.3 0.7 reduce.3
  71.0 0.1 reshape.265
  71.1 0.6 collective-permute-done
  71.8 1.2 pad_maximum_fusion
  73.0 42.3 %all-to-all-done.2 = f32[4,1024,256]{1,2,0:T(8,128)} async-done(((f32[4,1024,256]{1,2,0:T(8,128)}), f32[4,1024,256]{1,2,0:T(8,128)}, u32[]{:S(2)}, u32[]{:S(2)}) %all-to-all-start.2) | async-done | bytes 4194336 | tf_op jit(solution)/shard_map/all_to_all | solution.py:43
  115.4 2.0 %gather_fusion.1 = bf16[32,16,1152]{2,1,0:T(8,128)(2,1)S(1)} fusion(bf16[2,16,16,1152]{3,2,1,0:T(8,128)(2,1)} %pad_maximum_fusion, s32[32]{0:T(128)S(1)} %fusion.18), kind=kCustom, calls=%fused_computation.1 | custom fusion | bytes 2359552 | tf_op jit(solution)/shard_map/gather | solution.py:16
  117.4 1.2 broadcast_select_fusion
  118.6 4.5 %all-to-all-start.3 = ((bf16[4,8,16,1152]{3,2,1,0:T(8,128)(2,1)}), bf16[4,8,16,1152]{3,2,1,0:T(8,128)(2,1)S(1)}, u32[]{:S(2)}, u32[]{:S(2)}) async-start(bf16[4,8,16,1152]{3,2,1,0:T(8,128)(2,1)} %broadcast_select_fusion), calls=%async_computation.3 | async-start | bytes 2359296 | tf_op jit(solution)/shard_map/all_to_all | solution.py:65
  123.1 3.7 %reduce_sum.27 = f32[1024,256]{0,1:T(8,128)} reduce(f32[4,1024,256]{1,2,0:T(8,128)} %all-to-all-done.2, f32[]{:T(128)} %constant.75.clone.1), dimensions={0}, to_apply=%region_0.0 | reduce | flops 786432 | bytes 5242884 | tf_op jit(solution)/shard_map/reduce_sum | solution.py:61
  126.8 2.5 %copy.11 = f32[1024,256]{1,0:T(8,128)} copy(f32[1024,256]{0,1:T(8,128)} %reduce_sum.27) | data formatting | bytes 2097152 | tf_op jit(solution)/shard_map/reduce_sum | solution.py:61
  129.4 7.7 %all-to-all-done.3 = bf16[4,8,16,1152]{3,2,1,0:T(8,128)(2,1)S(1)} async-done(((bf16[4,8,16,1152]{3,2,1,0:T(8,128)(2,1)}), bf16[4,8,16,1152]{3,2,1,0:T(8,128)(2,1)S(1)}, u32[]{:S(2)}, u32[]{:S(2)}) %all-to-all-start.3) | async-done | bytes 1179680 | tf_op jit(solution)/shard_map/all_to_all | solution.py:65
  137.1 0.2 reduce_sum.28
  137.3 0.0 copy-start.2
  137.3 0.6 convolution_bitcast_fusion
  137.9 0.7 broadcast_in_dim.49
  138.7 3.4 %all-to-all-start.4 = ((f32[4,1024,16]{1,2,0:T(8,128)}), f32[4,1024,16]{1,2,0:T(8,128)S(1)}, u32[]{:S(2)}, u32[]{:S(2)}) async-start(f32[4,1024,16]{1,2,0:T(8,128)} %broadcast_in_dim.49), calls=%async_computation.4 | async-start | bytes 524288 | tf_op jit(solution)/shard_map/all_to_all | solution.py:77
  142.1 0.0 copy-done.2
  142.1 0.1 fusion.6
  142.2 6.6 %all-to-all-done.4 = f32[4,1024,16]{1,2,0:T(8,128)S(1)} async-done(((f32[4,1024,16]{1,2,0:T(8,128)}), f32[4,1024,16]{1,2,0:T(8,128)S(1)}, u32[]{:S(2)}, u32[]{:S(2)}) %all-to-all-start.4) | async-done | bytes 262176 | tf_op jit(solution)/shard_map/all_to_all | solution.py:77
  148.7 0.3 convolution_multiply_fusion
  149.1 1.0 fusion.1
  (10 shorter events, 0.1 us)
Async XLA Ops:
  0.0 7.9 %copy-start = (bf16[1024,896]{1,0:T(8,128)(2,1)S(1)}, bf16[1024,896]{1,0:T(8,128)(2,1)}, u32[]{:S(2)}) copy-start(bf16[1024,896]{1,0:T(8,128)(2,1)} %param.7) | copy-start | bytes 5505028
  2.7 11.1 %all-to-all-start = ((s32[4,1,8]{2,1,0:T(1,128)}), s32[4,1,8]{2,1,0:T(1,128)S(1)}, u32[]{:S(2)}, u32[]{:S(2)}) async-start(s32[4,1,8]{2,1,0:T(1,128)} %broadcast_in_dim.45), calls=%async_computation | async-start | bytes 4096 | tf_op jit(solution)/shard_map/all_to_all | solution.py:57
  63.0 52.3 %all-to-all-start.2 = ((f32[4,1024,256]{1,2,0:T(8,128)}), f32[4,1024,256]{1,2,0:T(8,128)}, u32[]{:S(2)}, u32[]{:S(2)}) async-start(f32[4,1024,256]{1,2,0:T(8,128)} %bitcast.40), calls=%async_computation.2 | async-start | bytes 8388608 | tf_op jit(solution)/shard_map/all_to_all | solution.py:43
  67.9 3.9 %collective-permute-start = (bf16[16,16,1152]{2,1,0:T(8,128)(2,1)S(1)}, bf16[16,16,1152]{2,1,0:T(8,128)(2,1)S(1)}, u32[]{:S(2)}, u32[]{:S(2)}) collective-permute-start(bf16[16,16,1152]{2,1,0:T(8,128)(2,1)S(1)} %bitcast.41), channel_id=1, source_target_pairs={{0,4},{4,0},{1,5},{5,1},{2,6},{6,2},{3,7},{7,3},{8,12},{12,8},{9,1... | collective-permute-start | bytes 1769480 | tf_op jit(solution)/shard_map/ppermute | solution.py:53
  118.6 18.5 %all-to-all-start.3 = ((bf16[4,8,16,1152]{3,2,1,0:T(8,128)(2,1)}), bf16[4,8,16,1152]{3,2,1,0:T(8,128)(2,1)S(1)}, u32[]{:S(2)}, u32[]{:S(2)}) async-start(bf16[4,8,16,1152]{3,2,1,0:T(8,128)(2,1)} %broadcast_select_fusion), calls=%async_computation.3 | async-start | bytes 2359296 | tf_op jit(solution)/shard_map/all_to_all | solution.py:65
  137.3 4.8 %copy-start.2 = (s32[8]{0:T(128)S(1)}, s32[8]{0:T(128)}, u32[]{:S(2)}) copy-start(s32[8]{0:T(128)} %param.12) | copy-start | bytes 100
  137.3 11.8 %copy-start.1 = (f32[1024,256]{1,0:T(8,128)S(1)}, f32[1024,256]{1,0:T(8,128)}, u32[]{:S(2)}) copy-start(f32[1024,256]{1,0:T(8,128)} %copy.11) | copy-start | bytes 3145732
  138.7 10.1 %all-to-all-start.4 = ((f32[4,1024,16]{1,2,0:T(8,128)}), f32[4,1024,16]{1,2,0:T(8,128)S(1)}, u32[]{:S(2)}, u32[]{:S(2)}) async-start(f32[4,1024,16]{1,2,0:T(8,128)} %broadcast_in_dim.49), calls=%async_computation.4 | async-start | bytes 524288 | tf_op jit(solution)/shard_map/all_to_all | solution.py:77
